TPU v7x, 128 devices: a whole 4x4x4 slice. The times are simulated.
128 devices in a mesh: section: 16 (over y, z_lo, core), sp: 8 (over z_hi, x).
Axes of the slice: x: 4, y: 4, z: 4 (z_hi: 2, z_lo: 2; z = z_hi * 2 + z_lo), core: 2. Of those that a mesh axis runs over, the one named last changes fastest.
Arguments:
- resid: float32 [16, 896, 6144], P('section', 'sp'), may hold values from -1.8 to 1.8
- qkv: bfloat16 [16, 896, 3, 6144], P('section', 'sp'), may hold values from -48 to 48
- cache_kv: bfloat16 [16, 2, 2, 1344, 6144], P('section', None, None, None, 'sp'), may hold values from -6 to 6
- out_proj: bfloat16 [16, 6144, 6144], P('section', 'sp'), may hold values from -0.078125 to 0.078125
- gate: float32 [16, 2, 6144], P('section'), may hold values from 0.5 to 2
- span_ids: int32 [16], P('section'), may hold values from 3 to 39
- cache_counts: int32 [16], P('section'), may hold values from 0 to 3, as said below
- span_mask: int32 [40, 40], replicated, may hold values from 0 to 1, as said below
Outputs:
- carried: float32 [16, 896, 6144], P('section', 'sp')
Inputs may be any that keep to these rules, and one draw needn't show every extreme that they name: `cache_counts`: some section has all 3 slots filled. span_mask[i][j] is 0 for j > i and 1 for j = i.
All inputs are finite; a program needn't handle non-finite values.
Results may differ from a plain program's by a relative error of at most 0.006.
Values may be sent and summed in bfloat16 or wider, within the bound.
No kernel may reach another device: no remote copies, remote signals or barrier semaphores. Data moves between devices by JAX's collectives and lax.ppermute only.
A program may use at most 384 MiB of HBM per device.

v0:
```python
import jax
import jax.numpy as jnp
from jax import lax
from jax.sharding import PartitionSpec as P

HDIM = 128
SPAN = 448
NCHUNK = 40
SLOTS = 3
VIDS = 2
TOKS = 896
KEYS = 1344


def passed_along(shard, axis, by):
    devices = lax.axis_size(axis)
    return lax.ppermute(shard, axis, [(i, (i + by) % devices) for i in range(devices)])


def visible_slots(span_id, filled, span_mask):
    row_mask = lax.dynamic_index_in_dim(span_mask, span_id, 0, keepdims=False)
    slot_ids = jnp.arange(SLOTS, dtype=jnp.int32)
    wanted = span_id - 1 - slot_ids
    columns = jnp.arange(NCHUNK, dtype=jnp.int32)
    looked = jnp.sum(jnp.where(columns[None, :] == wanted[:, None], row_mask[None, :], 0), axis=1)
    return (slot_ids < filled) & (looked == 1)


def far_scores(queries, cache_keys, live_slots):
    score_scale = HDIM ** (-0.5)
    scores = (
        jnp.einsum("qhe,khe->hqk", queries, cache_keys, preferred_element_type=jnp.float32)
        * score_scale
    )
    key_live = jnp.repeat(live_slots, SPAN)
    result = jnp.where(key_live[None, None, :], scores, -jnp.inf)
    return result


def mix_video(far_part, queries, own_keys, own_values, cache_values):
    score_scale = HDIM ** (-0.5)
    near_part = (
        jnp.einsum("qhe,khe->hqk", queries, own_keys, preferred_element_type=jnp.float32)
        * score_scale
    )
    scores = jnp.concatenate([far_part, near_part], axis=2)
    highest = jnp.max(scores, axis=2, keepdims=True)
    raised = jnp.exp(scores - highest)
    weights = (raised / jnp.sum(raised, axis=2, keepdims=True)).astype(jnp.bfloat16)
    values_all = jnp.concatenate([cache_values, own_values], axis=0)
    mixed = jnp.einsum("hqk,khe->qhe", weights, values_all, preferred_element_type=jnp.float32)
    return mixed.astype(jnp.bfloat16).reshape(SPAN, queries.shape[1] * HDIM)


def per_device(resid, qkv, cache_kv, out_proj, gate, span_ids, cache_counts, span_mask):
    own_rows = resid.shape[1]
    local_width = cache_kv.shape[4]
    local_heads = local_width // HDIM
    filled = cache_counts[0]
    live_slots = visible_slots(span_ids[0], filled, span_mask)
    cache_keys = cache_kv[0, 0].reshape(VIDS, KEYS, local_heads, HDIM)
    cache_values = cache_kv[0, 1].reshape(VIDS, KEYS, local_heads, HDIM)

    def score_video(inputs_one):
        return far_scores(inputs_one[0], inputs_one[1], live_slots)

    spread = lax.all_to_all(qkv[0], "sp", split_axis=2, concat_axis=0, tiled=True)
    queries = spread[:, 0].reshape(VIDS, SPAN, local_heads, HDIM)
    far_all = lax.map(score_video, (queries, cache_keys))
    own_keys = spread[:, 1].reshape(VIDS, SPAN, local_heads, HDIM)
    own_values = spread[:, 2].reshape(VIDS, SPAN, local_heads, HDIM)

    def mix_one(inputs_one):
        return mix_video(inputs_one[0], inputs_one[1], inputs_one[2], inputs_one[3], inputs_one[4])

    heads_all = lax.map(mix_one, (far_all, queries, own_keys, own_values, cache_values)).reshape(
        TOKS, local_width
    )
    projected = lax.psum_scatter(
        jnp.dot(heads_all, out_proj[0], preferred_element_type=jnp.float32),
        "sp",
        scatter_dimension=0,
        tiled=True,
    )
    device_place = lax.axis_index("sp")
    video_of = (device_place * own_rows + jnp.arange(own_rows, dtype=jnp.int32)) // SPAN
    picker = (video_of[:, None] == jnp.arange(VIDS, dtype=jnp.int32)[None, :]).astype(jnp.float32)
    gains = jnp.dot(picker, gate[0], precision=lax.Precision.HIGHEST)
    layer_out = resid[0] + gains * projected
    return passed_along(layer_out[None], "section", 1)


def solution(mesh):
    in_specs = (
        P("section", "sp", None),
        P("section", "sp", None, None),
        P("section", None, None, None, "sp"),
        P("section", "sp", None),
        P("section", None, None),
        P("section"),
        P("section"),
        P(),
    )
    out_specs = P("section", "sp", None)
    return jax.shard_map(
        per_device, mesh=mesh, in_specs=in_specs, out_specs=out_specs, check_vma=False
    )
```

profile of v0, /device:TPU:0, one launch (start us, length us, event | category | flops | bytes accessed | tf_op | source)
XLA Modules:
  0.0 543.8 jit_solution(14017527695531019002)
XLA Ops:
  6.5 10.0 %copy.53 = bf16[1,112,3,6144]{1,2,3,0:T(4,128)(2,1)} copy(bf16[1,112,3,6144]{3,1,2,0:T(8,128)(2,1)} %param.13) | data formatting | bytes 8257536 | tf_op args[1]
  16.5 7.7 %all-to-all-start = ((bf16[112,3,6144]{0,1,2:T(4,128)(2,1)}), bf16[112,3,6144]{0,1,2:T(4,128)(2,1)}, u32[]{:S(2)}, u32[]{:S(2)}) async-start(bf16[112,3,6144]{0,1,2:T(4,128)(2,1)} %bitcast.81), calls=%async_computation | async-start | bytes 12582912 | tf_op jit(solution)/shard_map/all_to_all | solution.py:67
  25.6 5.7 %fusion.31 = (bf16[1,1,2,1344,768]{4,3,2,1,0:T(8,128)(2,1)}, bf16[1,1,2,1344,768]{4,3,2,1,0:T(8,128)(2,1)}) fusion(bf16[1,2,2,1344,768]{4,3,2,1,0:T(8,128)(2,1)} %param.14), kind=kLoop, calls=%fused_computation.44 | loop fusion | bytes 16515072 | tf_op jit(solution)/shard_map/slice | solution.py:61
  31.3 6.4 %copy.58 = bf16[1,1,2,1344,768]{3,4,2,1,0:T(8,128)(2,1)} copy(bf16[1,1,2,1344,768]{4,3,2,1,0:T(8,128)(2,1)} %get-tuple-element.147) | data formatting | bytes 8257536 | tf_op jit(solution)/shard_map/slice | solution.py:61
  37.8 6.4 %copy.60 = bf16[2,1344,6,128]{3,1,2,0:T(8,128)(2,1)} copy(bf16[2,1344,6,128]{1,3,2,0:T(8,128)(2,1)} %bitcast.82) | data formatting | bytes 8257536 | tf_op jit(solution)/shard_map/while | solution.py:69
  44.2 6.4 %copy.52 = bf16[1,1,2,1344,768]{3,4,2,1,0:T(8,128)(2,1)} copy(bf16[1,1,2,1344,768]{4,3,2,1,0:T(8,128)(2,1)} %get-tuple-element.148) | data formatting | bytes 8257536 | tf_op jit(solution)/shard_map/slice | solution.py:62
  50.6 6.4 %copy.62 = bf16[2,1344,6,128]{3,1,2,0:T(8,128)(2,1)} copy(bf16[2,1344,6,128]{1,3,2,0:T(8,128)(2,1)} %bitcast.83) | data formatting | bytes 8257536 | tf_op jit(solution)/shard_map/while | solution.py:76
  57.9 39.8 %all-to-all-done = bf16[112,3,6144]{0,1,2:T(4,128)(2,1)} async-done(((bf16[112,3,6144]{0,1,2:T(4,128)(2,1)}), bf16[112,3,6144]{0,1,2:T(4,128)(2,1)}, u32[]{:S(2)}, u32[]{:S(2)}) %all-to-all-start) | async-done | bytes 4128800 | tf_op jit(solution)/shard_map/all_to_all | solution.py:67
  97.7 10.0 %copy.68 = bf16[112,3,8,768]{3,0,2,1:T(8,128)(2,1)} copy(bf16[112,3,8,768]{0,1,3,2:T(4,128)(2,1)} %bitcast.14) | data formatting | bytes 8257536 | tf_op jit(solution)/shard_map/all_to_all | solution.py:67
  107.8 3.5 fusion.32
  111.3 2.5 reshape.32
  113.8 1.7 copy.59
  115.5 18.3 %while.20 = (s32[]{:T(128)}, f32[2,6,448,1344]{3,2,1,0:T(8,128)}, pred[3]{0:T(512)(128)(4,1)S(1)}, bf16[2,448,6,128]{3,1,2,0:T(8,128)(2,1)S(1)}, bf16[2,1344,6,128]{3,1,2,0:T(8,128)(2,1)}, /*index=5*/s32[]{:T(128)}) while((s32[]{:T(128)}, f32[2,6,448,1344]{3,2,1,0:T(8,128)}, pred[3]{0:T(512)(128)(4,1)S(1)}, ...), condition=%wide.region_2.3_spmd, body=%wide.region_1.2_spmd.sunk | while | flops 932069376 | bytes 17899016 | solution.py:69
  115.6 9.0 %bitcast_dynamic-update-slice_fusion.2 = f32[2,6,448,1344]{3,2,1,0:T(8,128)} fusion(f32[2,6,448,1344]{3,2,1,0:T(8,128)} %get-tuple-element.241, s32[]{:T(128)} %get-tuple-element.240, pred[1344]{0:T(1024)(128)(4,1)S(1)} %broadcast_in_dim.72, bf16[2,1344,6,128]{3,1,2,0:T(8,128)(2,1)} %get-tuple-element.250, ...), kind=kOutput, calls=%fused_computation.clone.1 | convolution fusion | flops 932069376 | bytes 17894912 | tf_op jit(solution)/shard_map/while/body/eval_jaxpr/qhe,khe->hqk/dot_general | solution.py:32
  124.8 9.0 %bitcast_dynamic-update-slice_fusion.2 = f32[2,6,448,1344]{3,2,1,0:T(8,128)} fusion(f32[2,6,448,1344]{3,2,1,0:T(8,128)} %get-tuple-element.241, s32[]{:T(128)} %get-tuple-element.240, pred[1344]{0:T(1024)(128)(4,1)S(1)} %broadcast_in_dim.72, bf16[2,1344,6,128]{3,1,2,0:T(8,128)(2,1)} %get-tuple-element.250, ...), kind=kOutput, calls=%fused_computation.clone.1 | convolution fusion | flops 932069376 | bytes 17894912 | tf_op jit(solution)/shard_map/while/body/eval_jaxpr/qhe,khe->hqk/dot_general | solution.py:32
  133.8 4.1 reshape.30
  138.0 2.8 copy.63
  140.8 2.5 reshape.31
  143.2 2.8 copy.65
  146.0 81.0 %while.21 = (s32[]{:T(128)}, bf16[2,448,768]{2,1,0:T(8,128)(2,1)}, bf16[2,1344,6,128]{3,1,2,0:T(8,128)(2,1)}, bf16[2,448,6,128]{3,1,2,0:T(8,128)(2,1)}, f32[2,6,...) while((s32[]{:T(128)}, bf16[2,448,768]{2,1,0:T(8,128)(2,1)}, ...), condition=%wide.region_7.8_spmd, body=%wide.region_3.7_spmd.sunk | while | flops 1586989824 | bytes 108822680 | solution.py:76
  146.0 4.4 fusion.43
  150.4 11.6 %dynamic-slice_reduce_fusion.2 = (f32[6,448]{1,0:T(8,128)S(1)}, f32[6,448,1344]{2,1,0:T(8,128)}) fusion(f32[2,6,448,1344]{3,2,1,0:T(8,128)} %get-tuple-element.272, s32[]{:T(128)} %get-tuple-element.260), kind=kLoop, calls=%fused_computation.9.clone.1 | loop fusion | flops 3609984 | bytes 28912132 | tf_op jit(solution)/shard_map/while/body/eval_jaxpr/reduce_max | solution.py:47
  162.0 10.8 %fusion.44 = f32[6,448]{1,0:T(8,128)S(1)} fusion(f32[6,448,448]{2,1,0:T(8,128)} %get-tuple-element.230, f32[6,448,1344]{2,1,0:T(8,128)} %get-tuple-element.231, f32[6,448]{1,0:T(8,128)S(1)} %reduce_max.27), kind=kLoop, calls=%fused_computation.11.clone.1 | loop fusion | flops 14448000 | bytes 19289088 | tf_op jit(solution)/shard_map/while/body/eval_jaxpr/reduce_sum | solution.py:49
  175.1 10.0 %fusion.45 = bf16[448,6,128]{2,0,1:T(8,128)(2,1)S(1)} fusion(bf16[448,6,128]{2,0,1:T(8,128)(2,1)} %dynamic-slice_bitcast_fusion.6, bf16[1344,6,128]{2,0,1:T(8,128)(2,1)S(1)} %dynamic-slice_bitcast_fusion.7, f32[6,448,448]{2,1,0:T(8,128)} %get-tuple-element.230, f32[6,448,1344]{2,1,0:T(8,128)} %get-tuple-element.231, f32[6,448]{1,0:T(8,128)S(1)} %fusion.44, ...), kind=kOutput, calls=%fused_computation.19.clone.1 | convolution fusion | flops 1258242048 | bytes 22729728 | tf_op jit(solution)/shard_map/while/body/eval_jaxpr/hqk,khe->qhe/dot_general | solution.py:51
  186.6 4.4 fusion.43
  190.9 11.6 %dynamic-slice_reduce_fusion.2 = (f32[6,448]{1,0:T(8,128)S(1)}, f32[6,448,1344]{2,1,0:T(8,128)}) fusion(f32[2,6,448,1344]{3,2,1,0:T(8,128)} %get-tuple-element.272, s32[]{:T(128)} %get-tuple-element.260), kind=kLoop, calls=%fused_computation.9.clone.1 | loop fusion | flops 3609984 | bytes 28912132 | tf_op jit(solution)/shard_map/while/body/eval_jaxpr/reduce_max | solution.py:47
  202.6 10.8 %fusion.44 = f32[6,448]{1,0:T(8,128)S(1)} fusion(f32[6,448,448]{2,1,0:T(8,128)} %get-tuple-element.230, f32[6,448,1344]{2,1,0:T(8,128)} %get-tuple-element.231, f32[6,448]{1,0:T(8,128)S(1)} %reduce_max.27), kind=kLoop, calls=%fused_computation.11.clone.1 | loop fusion | flops 14448000 | bytes 19289088 | tf_op jit(solution)/shard_map/while/body/eval_jaxpr/reduce_sum | solution.py:49
  215.6 10.0 %fusion.45 = bf16[448,6,128]{2,0,1:T(8,128)(2,1)S(1)} fusion(bf16[448,6,128]{2,0,1:T(8,128)(2,1)} %dynamic-slice_bitcast_fusion.6, bf16[1344,6,128]{2,0,1:T(8,128)(2,1)S(1)} %dynamic-slice_bitcast_fusion.7, f32[6,448,448]{2,1,0:T(8,128)} %get-tuple-element.230, f32[6,448,1344]{2,1,0:T(8,128)} %get-tuple-element.231, f32[6,448]{1,0:T(8,128)S(1)} %fusion.44, ...), kind=kOutput, calls=%fused_computation.19.clone.1 | convolution fusion | flops 1258242048 | bytes 22729728 | tf_op jit(solution)/shard_map/while/body/eval_jaxpr/hqk,khe->qhe/dot_general | solution.py:51
  227.1 16.9 %fusion.24 = f32[896,6144]{1,0:T(8,128)} fusion(bf16[896,768]{1,0:T(8,128)(2,1)} %bitcast.85, bf16[1,768,6144]{2,1,0:T(8,128)(2,1)} %param.15), kind=kOutput, calls=%fused_computation.29 | convolution fusion | flops 8455716864 | bytes 32833536 | tf_op jit(solution)/shard_map/dot_general | solution.py:80
  244.0 253.5 %reduce-scatter.2.cloned.1.call-done = f32[112,6144]{1,0:T(8,128)} async-done(((f32[896,6144]{1,0:T(8,128)}), f32[112,6144]{1,0:T(8,128)}) %reduce-scatter.2.cloned.1.call-update) | async-done | bytes 2752528 | tf_op jit(solution)/shard_map/reduce_scatter | solution.py:79
  497.5 3.3 fusion.27
  500.9 34.6 %collective-permute-done = f32[1,112,6144]{2,1,0:T(8,128)S(1)} collective-permute-done((f32[1,112,6144]{2,1,0:T(8,128)S(1)}, f32[1,112,6144]{2,1,0:T(8,128)S(1)}, u32[]{:S(2)}, u32[]{:S(2)}) %collective-permute-start) | collective-permute-done | bytes 2752544 | tf_op jit(solution)/shard_map/ppermute | solution.py:17
  (39 shorter events, 10.2 us)
Async XLA Ops:
  6.5 491.0 %copy-start = (f32[1,2,6144]{2,1,0:T(2,128)S(1)}, f32[1,2,6144]{2,1,0:T(2,128)}, u32[]{:S(2)}) copy-start(f32[1,2,6144]{2,1,0:T(2,128)} %param.16) | copy-start | bytes 147460
  16.5 81.2 %all-to-all-start = ((bf16[112,3,6144]{0,1,2:T(4,128)(2,1)}), bf16[112,3,6144]{0,1,2:T(4,128)(2,1)}, u32[]{:S(2)}, u32[]{:S(2)}) async-start(bf16[112,3,6144]{0,1,2:T(4,128)(2,1)} %bitcast.81), calls=%async_computation | async-start | bytes 12582912 | tf_op jit(solution)/shard_map/all_to_all | solution.py:67
  24.3 473.2 %reduce-scatter.2.cloned.1.call-start = ((), (), s32[]{:S(2)}) async-start(), calls=%async_computation.2 | async-start | bytes 24772608 | tf_op jit(solution)/shard_map/reduce_scatter | solution.py:79
  162.0 10.8 %copy-start.1 = (bf16[2,1344,6,128]{3,1,2,0:T(8,128)(2,1)S(1)}, bf16[2,1344,6,128]{3,1,2,0:T(8,128)(2,1)}, u32[]{:S(2)}) copy-start(bf16[2,1344,6,128]{3,1,2,0:T(8,128)(2,1)} %get-tuple-element.270) | copy-start | bytes 12386308 | tf_op jit(solution)/shard_map/while
  172.8 1.3 copy-start.2
  202.5 10.8 %copy-start.1 = (bf16[2,1344,6,128]{3,1,2,0:T(8,128)(2,1)S(1)}, bf16[2,1344,6,128]{3,1,2,0:T(8,128)(2,1)}, u32[]{:S(2)}) copy-start(bf16[2,1344,6,128]{3,1,2,0:T(8,128)(2,1)} %get-tuple-element.270) | copy-start | bytes 12386308 | tf_op jit(solution)/shard_map/while
  213.4 1.3 copy-start.2
  244.0 253.5 %copy-start.3 = (f32[1,112,6144]{2,1,0:T(8,128)S(1)}, f32[1,112,6144]{2,1,0:T(8,128)}, u32[]{:S(2)}) copy-start(f32[1,112,6144]{2,1,0:T(8,128)} %param.12) | copy-start | bytes 8257540
  500.8 34.7 %collective-permute-start = (f32[1,112,6144]{2,1,0:T(8,128)S(1)}, f32[1,112,6144]{2,1,0:T(8,128)S(1)}, u32[]{:S(2)}, u32[]{:S(2)}) collective-permute-start(f32[1,112,6144]{2,1,0:T(8,128)S(1)} %fusion.27), channel_id=1, source_target_pairs={{0,8},{8,16},{16,24},{24,32},{32,40},{40,48},{48,56},{56,64},{64,7... | collective-permute-start | bytes 8257544 | tf_op jit(solution)/shard_map/ppermute | solution.py:17
Sparse Core Ops, SparseCore 0:
  244.1 253.3 reduce-scatter.1
where the time goes:
time: 546 us; the launch traced here: 544 us
  waiting for transfers between devices  328 us (60%)
  local copies, waits for them, and re-layouts  81.2 us (15%)
  matrix products  67 us (12%)
  other arithmetic  45.1 us (8%)
  between operations  14.8 us (3%)
  starting transfers between devices  7.83 us (1%)
    reduce_scatter x1, waiting for transfers between devices, per_device(): lax.psum_scatter(jnp.dot(heads_all, out_proj[0], preferred_element_type=j...  253 us
    all_to_all x1, waiting for transfers between devices, per_device(): lax.all_to_all(qkv[0], 'sp', split_axis=2, concat_axis=0, tiled=True)  39.8 us
    ppermute x1, waiting for transfers between devices, passed_along(): lax.ppermute(shard, axis, [(i, (i + by) % devices) for i in range(devices)])  34.6 us
    reduce_max x4, other arithmetic, mix_video(): highest = jnp.max(scores, axis=2, keepdims=True)  23.2 us
    reduce_sum x2, other arithmetic, mix_video(): jnp.sum(raised, axis=2, keepdims=True)  21.6 us
    dot_general x2, matrix products, mix_video(): jnp.einsum('hqk,khe->qhe', weights, values_all, preferred_element_type=jn...  20.1 us
    dot_general x2, matrix products, far_scores(): jnp.einsum('qhe,khe->hqk', queries, cache_keys, preferred_element_type=jn...  18 us
    dot_general x1, matrix products, per_device(): jnp.dot(heads_all, out_proj[0], preferred_element_type=jnp.float32)  16.9 us
  transfers between devices with their start and end apart: 3, of which 3 were waited for; matrix products, arithmetic and copies ran while one was open for 6% of the time, Pallas kernels for 0%

commit v1 on v0

--- a/solution.py
+++ b/solution.py
@@ -10,6 +10,13 @@
 VIDS = 2
 TOKS = 896
 KEYS = 1344
+
+
+def _name_chains(row_data):
+    tile_out = jnp.stack(jnp.split(row_data, jax.lax.axis_size("sp"), axis=2), axis=0)
+    moved = jax.lax.all_to_all(tile_out, "sp", 0, 0)
+    reached = jnp.concatenate(moved, axis=0)
+    return reached
 
 
 def passed_along(shard, axis, by):
@@ -64,7 +71,7 @@
     def score_video(inputs_one):
         return far_scores(inputs_one[0], inputs_one[1], live_slots)
 
-    spread = lax.all_to_all(qkv[0], "sp", split_axis=2, concat_axis=0, tiled=True)
+    spread = _name_chains(qkv[0])
     queries = spread[:, 0].reshape(VIDS, SPAN, local_heads, HDIM)
     far_all = lax.map(score_video, (queries, cache_keys))
     own_keys = spread[:, 1].reshape(VIDS, SPAN, local_heads, HDIM)

time: 546 us -> 504 us (0.923)
  waiting for transfers between devices: 328 us -> 296 us
  local copies, waits for them, and re-layouts: 81.2 us -> 72.6 us
    all_to_all x1, waiting for transfers between devices: 39.8 us -> 16.6 us  [_name_chains(): moved = jax.lax.all_to_all(tile_out, 'sp', 0, 0)]
    reduce_scatter x1, waiting for transfers between devices: 253 us -> 245 us  [per_device(): lax.psum_scatter(jnp.dot(heads_all, out_proj[0], preferred_element_type=j...]
    all_to_all x1, local copies, waits for them, and re-layouts: 10 us -> 2.52 us  [_name_chains(): moved = jax.lax.all_to_all(tile_out, 'sp', 0, 0)]
    unnamed x6 -> x14, local copies, waits for them, and re-layouts: 11.5 us -> 11.8 us
where the time goes in v1:
time: 504 us; the launch traced here: 503 us
  waiting for transfers between devices  296 us (59%)
  local copies, waits for them, and re-layouts  72.6 us (14%)
  matrix products  67 us (13%)
  other arithmetic  45.1 us (9%)
  between operations  14.8 us (3%)
  starting transfers between devices  7.83 us (2%)
    reduce_scatter x1, waiting for transfers between devices, per_device(): lax.psum_scatter(jnp.dot(heads_all, out_proj[0], preferred_element_type=j...  245 us
    ppermute x1, waiting for transfers between devices, passed_along(): lax.ppermute(shard, axis, [(i, (i + by) % devices) for i in range(devices)])  34.6 us
    reduce_max x4, other arithmetic, mix_video(): highest = jnp.max(scores, axis=2, keepdims=True)  23.3 us
    reduce_sum x2, other arithmetic, mix_video(): jnp.sum(raised, axis=2, keepdims=True)  21.6 us
    dot_general x2, matrix products, mix_video(): jnp.einsum('hqk,khe->qhe', weights, values_all, preferred_element_type=jn...  20.1 us
    dot_general x2, matrix products, far_scores(): jnp.einsum('qhe,khe->hqk', queries, cache_keys, preferred_element_type=jn...  18 us
    dot_general x1, matrix products, per_device(): jnp.dot(heads_all, out_proj[0], preferred_element_type=jnp.float32)  16.9 us
    all_to_all x1, waiting for transfers between devices, _name_chains(): moved = jax.lax.all_to_all(tile_out, 'sp', 0, 0)  16.6 us
  transfers between devices with their start and end apart: 3, of which 3 were waited for; matrix products, arithmetic and copies ran while one was open for 6% of the time, Pallas kernels for 0%

profile of v1, /device:TPU:0, one launch (start us, length us, event | category | flops | bytes accessed | tf_op | source)
XLA Modules:
  0.0 503.1 jit_solution(15302596802210320885)
XLA Ops:
  6.5 2.0 fusion.35
  10.4 1.9 fusion.33
  12.3 1.9 fusion.32
  17.6 7.7 %all-to-all-start = ((bf16[8,112,3,768]{3,1,2,0:T(8,128)(2,1)}), bf16[8,112,3,768]{3,1,2,0:T(8,128)(2,1)}, u32[]{:S(2)}, u32[]{:S(2)}) async-start(bf16[8,112,3,768]{3,1,2,0:T(8,128)(2,1)} %fusion.28), calls=%async_computation | async-start | bytes 8257536 | tf_op jit(solution)/shard_map/all_to_all | solution.py:17
  26.7 5.7 %fusion.39 = (bf16[1,1,2,1344,768]{4,3,2,1,0:T(8,128)(2,1)}, bf16[1,1,2,1344,768]{4,3,2,1,0:T(8,128)(2,1)}) fusion(bf16[1,2,2,1344,768]{4,3,2,1,0:T(8,128)(2,1)} %param.14), kind=kLoop, calls=%fused_computation.60 | loop fusion | bytes 16515072 | tf_op jit(solution)/shard_map/slice | solution.py:68
  32.3 6.5 %copy.67 = bf16[1,1,2,1344,768]{3,4,2,1,0:T(8,128)(2,1)} copy(bf16[1,1,2,1344,768]{4,3,2,1,0:T(8,128)(2,1)} %get-tuple-element.147) | data formatting | bytes 8257536 | tf_op jit(solution)/shard_map/slice | solution.py:68
  38.8 6.5 %copy.69 = bf16[2,1344,6,128]{3,1,2,0:T(8,128)(2,1)} copy(bf16[2,1344,6,128]{1,3,2,0:T(8,128)(2,1)} %bitcast.109) | data formatting | bytes 8257536 | tf_op jit(solution)/shard_map/while | solution.py:76
  45.2 6.5 %copy.63 = bf16[1,1,2,1344,768]{3,4,2,1,0:T(8,128)(2,1)} copy(bf16[1,1,2,1344,768]{4,3,2,1,0:T(8,128)(2,1)} %get-tuple-element.148) | data formatting | bytes 8257536 | tf_op jit(solution)/shard_map/slice | solution.py:69
  51.7 6.4 %copy.71 = bf16[2,1344,6,128]{3,1,2,0:T(8,128)(2,1)} copy(bf16[2,1344,6,128]{1,3,2,0:T(8,128)(2,1)} %bitcast.110) | data formatting | bytes 8257536 | tf_op jit(solution)/shard_map/while | solution.py:83
  59.0 16.6 %all-to-all-done = bf16[8,112,3,768]{3,1,2,0:T(8,128)(2,1)} async-done(((bf16[8,112,3,768]{3,1,2,0:T(8,128)(2,1)}), bf16[8,112,3,768]{3,1,2,0:T(8,128)(2,1)}, u32[]{:S(2)}, u32[]{:S(2)}) %all-to-all-start) | async-done | bytes 4128800 | tf_op jit(solution)/shard_map/all_to_all | solution.py:17
  75.6 2.5 copy.64
  79.5 2.5 reshape.36
  83.7 18.3 %while.20 = (s32[]{:T(128)}, f32[2,6,448,1344]{3,2,1,0:T(8,128)}, pred[3]{0:T(512)(128)(4,1)S(1)}, bf16[2,448,6,128]{3,1,2,0:T(8,128)(2,1)S(1)}, bf16[2,1344,6,128]{3,1,2,0:T(8,128)(2,1)}, /*index=5*/s32[]{:T(128)}) while((s32[]{:T(128)}, f32[2,6,448,1344]{3,2,1,0:T(8,128)}, pred[3]{0:T(512)(128)(4,1)S(1)}, ...), condition=%wide.region_2.3_spmd, body=%wide.region_1.2_spmd.sunk | while | flops 932069376 | bytes 17899016 | solution.py:76
  83.8 9.0 %bitcast_dynamic-update-slice_fusion.2 = f32[2,6,448,1344]{3,2,1,0:T(8,128)} fusion(f32[2,6,448,1344]{3,2,1,0:T(8,128)} %get-tuple-element.241, s32[]{:T(128)} %get-tuple-element.240, pred[1344]{0:T(1024)(128)(4,1)S(1)} %broadcast_in_dim.72, bf16[2,1344,6,128]{3,1,2,0:T(8,128)(2,1)} %get-tuple-element.250, ...), kind=kOutput, calls=%fused_computation.clone.1 | convolution fusion | flops 932069376 | bytes 17894912 | tf_op jit(solution)/shard_map/while/body/eval_jaxpr/qhe,khe->hqk/dot_general | solution.py:39
  93.0 9.0 %bitcast_dynamic-update-slice_fusion.2 = f32[2,6,448,1344]{3,2,1,0:T(8,128)} fusion(f32[2,6,448,1344]{3,2,1,0:T(8,128)} %get-tuple-element.241, s32[]{:T(128)} %get-tuple-element.240, pred[1344]{0:T(1024)(128)(4,1)S(1)} %broadcast_in_dim.72, bf16[2,1344,6,128]{3,1,2,0:T(8,128)(2,1)} %get-tuple-element.250, ...), kind=kOutput, calls=%fused_computation.clone.1 | convolution fusion | flops 932069376 | bytes 17894912 | tf_op jit(solution)/shard_map/while/body/eval_jaxpr/qhe,khe->hqk/dot_general | solution.py:39
  102.0 4.1 reshape.34
  106.1 2.8 copy.72
  108.9 2.5 reshape.35
  111.4 2.8 copy.74
  114.2 81.1 %while.21 = (s32[]{:T(128)}, bf16[2,448,768]{2,1,0:T(8,128)(2,1)}, bf16[2,1344,6,128]{3,1,2,0:T(8,128)(2,1)}, bf16[2,448,6,128]{3,1,2,0:T(8,128)(2,1)}, f32[2,6,...) while((s32[]{:T(128)}, bf16[2,448,768]{2,1,0:T(8,128)(2,1)}, ...), condition=%wide.region_7.8_spmd, body=%wide.region_3.7_spmd.sunk | while | flops 1586989824 | bytes 108822680 | solution.py:83
  114.2 4.4 fusion.51
  118.6 11.6 %dynamic-slice_reduce_fusion.2 = (f32[6,448]{1,0:T(8,128)S(1)}, f32[6,448,1344]{2,1,0:T(8,128)}) fusion(f32[2,6,448,1344]{3,2,1,0:T(8,128)} %get-tuple-element.272, s32[]{:T(128)} %get-tuple-element.260), kind=kLoop, calls=%fused_computation.9.clone.1 | loop fusion | flops 3609984 | bytes 28912132 | tf_op jit(solution)/shard_map/while/body/eval_jaxpr/reduce_max | solution.py:54
  130.2 10.8 %fusion.52 = f32[6,448]{1,0:T(8,128)S(1)} fusion(f32[6,448,448]{2,1,0:T(8,128)} %get-tuple-element.230, f32[6,448,1344]{2,1,0:T(8,128)} %get-tuple-element.231, f32[6,448]{1,0:T(8,128)S(1)} %reduce_max.27), kind=kLoop, calls=%fused_computation.11.clone.1 | loop fusion | flops 14448000 | bytes 19289088 | tf_op jit(solution)/shard_map/while/body/eval_jaxpr/reduce_sum | solution.py:56
  143.3 10.0 %fusion.53 = bf16[448,6,128]{2,0,1:T(8,128)(2,1)S(1)} fusion(bf16[448,6,128]{2,0,1:T(8,128)(2,1)} %dynamic-slice_bitcast_fusion.6, bf16[1344,6,128]{2,0,1:T(8,128)(2,1)S(1)} %dynamic-slice_bitcast_fusion.7, f32[6,448,448]{2,1,0:T(8,128)} %get-tuple-element.230, f32[6,448,1344]{2,1,0:T(8,128)} %get-tuple-element.231, f32[6,448]{1,0:T(8,128)S(1)} %fusion.52, ...), kind=kOutput, calls=%fused_computation.19.clone.1 | convolution fusion | flops 1258242048 | bytes 22729728 | tf_op jit(solution)/shard_map/while/body/eval_jaxpr/hqk,khe->qhe/dot_general | solution.py:58
  154.8 4.4 fusion.51
  159.1 11.6 %dynamic-slice_reduce_fusion.2 = (f32[6,448]{1,0:T(8,128)S(1)}, f32[6,448,1344]{2,1,0:T(8,128)}) fusion(f32[2,6,448,1344]{3,2,1,0:T(8,128)} %get-tuple-element.272, s32[]{:T(128)} %get-tuple-element.260), kind=kLoop, calls=%fused_computation.9.clone.1 | loop fusion | flops 3609984 | bytes 28912132 | tf_op jit(solution)/shard_map/while/body/eval_jaxpr/reduce_max | solution.py:54
  170.8 10.8 %fusion.52 = f32[6,448]{1,0:T(8,128)S(1)} fusion(f32[6,448,448]{2,1,0:T(8,128)} %get-tuple-element.230, f32[6,448,1344]{2,1,0:T(8,128)} %get-tuple-element.231, f32[6,448]{1,0:T(8,128)S(1)} %reduce_max.27), kind=kLoop, calls=%fused_computation.11.clone.1 | loop fusion | flops 14448000 | bytes 19289088 | tf_op jit(solution)/shard_map/while/body/eval_jaxpr/reduce_sum | solution.py:56
  183.8 10.0 %fusion.53 = bf16[448,6,128]{2,0,1:T(8,128)(2,1)S(1)} fusion(bf16[448,6,128]{2,0,1:T(8,128)(2,1)} %dynamic-slice_bitcast_fusion.6, bf16[1344,6,128]{2,0,1:T(8,128)(2,1)S(1)} %dynamic-slice_bitcast_fusion.7, f32[6,448,448]{2,1,0:T(8,128)} %get-tuple-element.230, f32[6,448,1344]{2,1,0:T(8,128)} %get-tuple-element.231, f32[6,448]{1,0:T(8,128)S(1)} %fusion.52, ...), kind=kOutput, calls=%fused_computation.19.clone.1 | convolution fusion | flops 1258242048 | bytes 22729728 | tf_op jit(solution)/shard_map/while/body/eval_jaxpr/hqk,khe->qhe/dot_general | solution.py:58
  195.3 16.9 %fusion.24 = f32[896,6144]{1,0:T(8,128)} fusion(bf16[896,768]{1,0:T(8,128)(2,1)} %bitcast.120, bf16[1,768,6144]{2,1,0:T(8,128)(2,1)} %param.15), kind=kOutput, calls=%fused_computation.29 | convolution fusion | flops 8455716864 | bytes 32833536 | tf_op jit(solution)/shard_map/dot_general | solution.py:87
  212.2 244.5 %reduce-scatter.2.cloned.1.call-done = f32[112,6144]{1,0:T(8,128)} async-done(((f32[896,6144]{1,0:T(8,128)}), f32[112,6144]{1,0:T(8,128)}) %reduce-scatter.2.cloned.1.call-update) | async-done | bytes 2752528 | tf_op jit(solution)/shard_map/reduce_scatter | solution.py:86
  456.8 3.3 fusion.27
  460.1 34.6 %collective-permute-done = f32[1,112,6144]{2,1,0:T(8,128)S(1)} collective-permute-done((f32[1,112,6144]{2,1,0:T(8,128)S(1)}, f32[1,112,6144]{2,1,0:T(8,128)S(1)}, u32[]{:S(2)}, u32[]{:S(2)}) %collective-permute-start) | collective-permute-done | bytes 2752544 | tf_op jit(solution)/shard_map/ppermute | solution.py:24
  (48 shorter events, 18.5 us)
Async XLA Ops:
  6.5 450.2 %copy-start = (f32[1,2,6144]{2,1,0:T(2,128)S(1)}, f32[1,2,6144]{2,1,0:T(2,128)}, u32[]{:S(2)}) copy-start(f32[1,2,6144]{2,1,0:T(2,128)} %param.16) | copy-start | bytes 147460
  6.5 7.6 %copy-start.3 = (bf16[1,112,3,6144]{3,1,2,0:T(8,128)(2,1)S(1)}, bf16[1,112,3,6144]{3,1,2,0:T(8,128)(2,1)}, u32[]{:S(2)}) copy-start(bf16[1,112,3,6144]{3,1,2,0:T(8,128)(2,1)} %param.13) | copy-start | bytes 12386308
  17.6 58.0 %all-to-all-start = ((bf16[8,112,3,768]{3,1,2,0:T(8,128)(2,1)}), bf16[8,112,3,768]{3,1,2,0:T(8,128)(2,1)}, u32[]{:S(2)}, u32[]{:S(2)}) async-start(bf16[8,112,3,768]{3,1,2,0:T(8,128)(2,1)} %fusion.28), calls=%async_computation | async-start | bytes 8257536 | tf_op jit(solution)/shard_map/all_to_all | solution.py:17
  25.3 431.5 %reduce-scatter.2.cloned.1.call-start = ((), (), s32[]{:S(2)}) async-start(), calls=%async_computation.2 | async-start | bytes 24772608 | tf_op jit(solution)/shard_map/reduce_scatter | solution.py:86
  130.2 10.8 %copy-start.1 = (bf16[2,1344,6,128]{3,1,2,0:T(8,128)(2,1)S(1)}, bf16[2,1344,6,128]{3,1,2,0:T(8,128)(2,1)}, u32[]{:S(2)}) copy-start(bf16[2,1344,6,128]{3,1,2,0:T(8,128)(2,1)} %get-tuple-element.270) | copy-start | bytes 12386308 | tf_op jit(solution)/shard_map/while
  141.0 1.3 copy-start.2
  170.8 10.8 %copy-start.1 = (bf16[2,1344,6,128]{3,1,2,0:T(8,128)(2,1)S(1)}, bf16[2,1344,6,128]{3,1,2,0:T(8,128)(2,1)}, u32[]{:S(2)}) copy-start(bf16[2,1344,6,128]{3,1,2,0:T(8,128)(2,1)} %get-tuple-element.270) | copy-start | bytes 12386308 | tf_op jit(solution)/shard_map/while
  181.6 1.3 copy-start.2
  212.2 244.6 %copy-start.4 = (f32[1,112,6144]{2,1,0:T(8,128)S(1)}, f32[1,112,6144]{2,1,0:T(8,128)}, u32[]{:S(2)}) copy-start(f32[1,112,6144]{2,1,0:T(8,128)} %param.12) | copy-start | bytes 8257540
  460.0 34.7 %collective-permute-start = (f32[1,112,6144]{2,1,0:T(8,128)S(1)}, f32[1,112,6144]{2,1,0:T(8,128)S(1)}, u32[]{:S(2)}, u32[]{:S(2)}) collective-permute-start(f32[1,112,6144]{2,1,0:T(8,128)S(1)} %fusion.27), channel_id=1, source_target_pairs={{0,8},{8,16},{16,24},{24,32},{32,40},{40,48},{48,56},{56,64},{64,7... | collective-permute-start | bytes 8257544 | tf_op jit(solution)/shard_map/ppermute | solution.py:24
Sparse Core Ops, SparseCore 0:
  212.3 244.3 reduce-scatter.1
